TPU v7x, 32 devices: a whole 2x2x4 slice. The times are simulated.
32 devices in a mesh: mp: 2 (over y), tx: 4 (over z), ty: 4 (over x, core).
Axes of the slice: x: 2, y: 2, z: 4, core: 2. Of those that a mesh axis runs over, the one named last changes fastest.
Arguments:
- models: float32 [2, 16, 64, 512], P('mp', None, 'ty', 'tx'), may hold values from -6 to 6
- direction: float32 [2, 16, 64, 512], P('mp', None, 'ty', 'tx'), may hold values from -6 to 6
- coupling: float32 [2], replicated, may hold values from 0.1 to 0.4
- tv_weight: float32 [2], replicated, may hold values from 0.5 to 2
Outputs:
- gradient: float32 [2, 16, 64, 512], P('mp', None, 'ty', 'tx')
- hessian_vector: float32 [2, 16, 64, 512], P('mp', None, 'ty', 'tx')
All inputs are finite; a program needn't handle non-finite values.
Results may differ from a plain program's by a relative error of at most 0.0001.
Values sent between devices are 32-bit elements; how exact they have to be, the bound alone decides.
No kernel may reach another device: no remote copies, remote signals or barrier semaphores. Data moves between devices by JAX's collectives and lax.ppermute only.
A program may use at most 64 MiB of HBM per device.

v0:
```python
import jax
import jax.numpy as jnp
from jax import lax
from jax.sharding import PartitionSpec as P

EPS_SQ = 0.25
SYM_PAIRS = ((0, 0), (1, 1), (2, 2), (0, 1), (0, 2), (1, 2))


def passed_along(array, axis, by):
    size = lax.axis_size(axis)
    pairs = [(i, i + by) for i in range(size) if 0 <= i + by < size]
    return lax.ppermute(array, axis, pairs)


def edge_masks(width_y, width_x):
    end_x = lax.axis_index("tx") == lax.axis_size("tx") - 1
    end_y = lax.axis_index("ty") == lax.axis_size("ty") - 1
    col_x = lax.broadcasted_iota(jnp.int32, (1, 1, width_x), 2)
    row_y = lax.broadcasted_iota(jnp.int32, (1, width_y, 1), 1)
    return ((col_x == width_x - 1) & end_x, (row_y == width_y - 1) & end_y)


def fields(tile, rim_x, rim_y):
    last_x, last_y = edge_masks(tile.shape[3], tile.shape[4])
    dx = jnp.concatenate([tile[..., 1:], rim_x], -1) - tile
    dx = jnp.where(last_x, 0.0, dx)
    dy = jnp.concatenate([tile[..., 1:, :], rim_y], -2) - tile
    dy = jnp.where(last_y, 0.0, dy)
    dz = jnp.concatenate(
        [tile[..., 1:, :, :] - tile[..., :-1, :, :], jnp.zeros_like(tile[..., :1, :, :])], -3
    )
    grads = jnp.stack([dx[:, 0], dy[:, 0], dz[:, 0]], 1)
    dirs = jnp.stack([dx[:, 1], dy[:, 1], dz[:, 1]], 1)
    return (grads, dirs)


def moments(grads, dirs, weights):
    wts = weights[:, None, None, None]
    rows = [jnp.sum(wts * grads[:, i] * grads[:, j], 0) for i, j in SYM_PAIRS]
    for i in range(3):
        for j in range(3):
            rows.append(jnp.sum(wts * dirs[:, i] * grads[:, j], 0))
    return jnp.stack(rows, 0)


def couple(moms, grad_own, dir_own):
    trace_m = moms[0] + moms[1] + moms[2]
    mat = [[moms[0], moms[3], moms[4]], [moms[3], moms[1], moms[5]], [moms[4], moms[5], moms[2]]]
    nat = [[moms[6 + 3 * i + j] for j in range(3)] for i in range(3)]
    trace_n = nat[0][0] + nat[1][1] + nat[2][2]
    g_parts = [grad_own[..., i, :, :, :] for i in range(3)]
    e_parts = [dir_own[..., i, :, :, :] for i in range(3)]
    cross_q = []
    cross_p = []
    for i in range(3):
        mg = mat[i][0] * g_parts[0] + mat[i][1] * g_parts[1] + mat[i][2] * g_parts[2]
        me = mat[i][0] * e_parts[0] + mat[i][1] * e_parts[1] + mat[i][2] * e_parts[2]
        ng = nat[i][0] * g_parts[0] + nat[i][1] * g_parts[1] + nat[i][2] * g_parts[2]
        cross_q.append(trace_m * g_parts[i] - mg)
        cross_p.append(trace_m * e_parts[i] - me + trace_n * g_parts[i] - ng)
    return (jnp.stack(cross_q, axis=-4), jnp.stack(cross_p, axis=-4))


def model_split(own, rim_x, rim_y, alpha, beta, own_weights):
    grads, dirs = fields(own, rim_x, rim_y)
    moms = lax.psum(moments(grads, dirs, own_weights), "mp")
    grad_own = grads[0]
    dir_own = dirs[0]
    cross_q, cross_p = couple(moms, grad_own, dir_own)
    size = jnp.sqrt(jnp.sum(grad_own * grad_own, 0) + EPS_SQ)[None]
    flux = jnp.stack(
        [beta * grad_own / size + alpha * cross_q, beta * dir_own / size + alpha * cross_p], 0
    )
    last_x, last_y = edge_masks(flux.shape[3], flux.shape[4])
    flux_x = jnp.where(last_x, 0.0, flux[:, 0])
    flux_y = jnp.where(last_y, 0.0, flux[:, 1])
    flux_z = flux[:, 2]
    flux_z = jnp.concatenate([flux_z[..., :-1, :, :], jnp.zeros_like(flux_z[..., :1, :, :])], -3)
    prev_x = passed_along(flux_x[..., -1:], "tx", 1)
    prev_y = passed_along(flux_y[..., -1:, :], "ty", 1)
    result = jnp.concatenate([prev_x, flux_x[..., :-1]], -1) - flux_x
    result = result + jnp.concatenate([prev_y, flux_y[..., :-1, :]], -2) - flux_y
    result = (
        result
        + jnp.concatenate([jnp.zeros_like(flux_z[..., :1, :, :]), flux_z[..., :-1, :, :]], -3)
        - flux_z
    )
    return (result[0][None], result[1][None])


def shards(models, direction, coupling, tv_weight):
    member = lax.axis_index("mp")
    own_weights = lax.dynamic_slice_in_dim(coupling, member, 1)
    alpha = own_weights[0]
    beta = lax.dynamic_slice_in_dim(tv_weight, member, 1)[0]
    own = jnp.stack([models, direction], 1)
    rim_x = passed_along(own[..., :1], "tx", -1)
    rim_y = passed_along(own[..., :1, :], "ty", -1)
    return model_split(own, rim_x, rim_y, alpha, beta, own_weights)


def solution(mesh):
    placed = (P("mp", None, "ty", "tx"), P("mp", None, "ty", "tx"), P(), P())
    return jax.shard_map(
        shards,
        mesh=mesh,
        in_specs=placed,
        out_specs=(P("mp", None, "ty", "tx"), P("mp", None, "ty", "tx")),
        check_vma=False,
    )
```

profile of v0, /device:TPU:0, one launch (start us, length us, event | category | flops | bytes accessed | tf_op | source)
XLA Modules:
  0.0 117.1 jit_solution(6490164148567552637)
XLA Ops:
  7.2 0.9 fusion.75
  8.2 1.3 %collective-permute-start.1 = (f32[1,2,16,1,128]{4,3,2,1,0:T(1,128)S(1)}, f32[1,2,16,1,128]{4,3,2,1,0:T(1,128)S(1)}, u32[]{:S(2)}, u32[]{:S(2)}) collective-permute-start(f32[1,2,16,1,128]{4,3,2,1,0:T(1,128)S(1)} %fusion.75), channel_id=1, source_target_pairs={{1,0},{2,1},{3,2},{5,4},{6,5},{7,6},{9,8},{10,9},{11,10},{13,12},{... | collective-permute-start | bytes 49160 | tf_op jit(solution)/shard_map/ppermute | solution.py:13
  9.5 1.0 fusion.6
  10.5 1.3 %collective-permute-start = (f32[1,2,16,16,1]{4,3,2,1,0:T(8,128)S(1)}, f32[1,2,16,16,1]{4,3,2,1,0:T(8,128)S(1)}, u32[]{:S(2)}, u32[]{:S(2)}) collective-permute-start(f32[1,2,16,16,1]{4,3,2,1,0:T(8,128)S(1)} %fusion.6), channel_id=1, source_target_pairs={{4,0},{8,4},{12,8},{5,1},{9,5},{13,9},{6,2},{10,6},{14,10},{7,3},{... | collective-permute-start | bytes 6152 | tf_op jit(solution)/shard_map/ppermute | solution.py:13
  11.8 1.0 fusion.7
  12.8 1.1 fusion.5
  13.9 1.1 fusion.22
  15.6 6.5 %collective-permute-done = f32[1,2,16,16,1]{4,3,2,1,0:T(8,128)S(1)} collective-permute-done((f32[1,2,16,16,1]{4,3,2,1,0:T(8,128)S(1)}, f32[1,2,16,16,1]{4,3,2,1,0:T(8,128)S(1)}, u32[]{:S(2)}, u32[]{:S(2)}) %collective-permute-start) | collective-permute-done | bytes 2080 | tf_op jit(solution)/shard_map/ppermute | solution.py:13
  22.3 0.7 fusion.24
  23.0 0.7 fusion.27
  23.7 0.7 fusion.29
  24.3 0.7 fusion.25
  25.0 0.7 fusion.26
  25.7 0.7 fusion.28
  26.3 0.7 fusion.72
  27.0 0.7 fusion.66
  27.7 0.7 fusion.54
  28.4 0.7 fusion.73
  29.0 0.7 fusion.67
  29.7 0.7 fusion.55
  30.4 0.7 fusion.74
  31.1 0.7 fusion.68
  31.7 0.7 fusion.56
  32.4 1.3 %copy-done.3 = f32[15,16,16,128]{3,2,1,0:T(8,128)} copy-done((f32[15,16,16,128]{3,2,1,0:T(8,128)}, f32[15,16,16,128]{3,2,1,0:T(8,128)S(1)}, u32[]{:S(2)}) %copy-start.3) | copy-done | bytes 1966104
  34.4 60.8 %all-reduce.4.cloned.1.call-done = f32[15,16,16,128]{3,2,1,0:T(8,128)} async-done(((f32[15,16,16,128]{3,2,1,0:T(8,128)}), f32[15,16,16,128]{3,2,1,0:T(8,128)}) %all-reduce.4.cloned.1.call-update) | async-done | bytes 1966096 | tf_op jit(solution)/shard_map/psum | solution.py:67
  95.2 1.6 %fusion.40 = (f32[1,1,16,16,128]{4,3,2,0,1:T(8,128)S(1)}, f32[1,16,16,128]{3,2,1,0:T(8,128)S(1)}, f32[1,16,16,128]{3,2,1,0:T(8,128)S(1)}) fusion(f32[15,16,16,128]{3,2,1,0:T(8,128)} %all-reduce.4.cloned.1.call-done, f32[1,2,16,16,128]{4,3,2,1,0:T(8,128)S(1)} %get-tuple-element.17, f32[1,2,16,16,128]{4,3,2,1,0:T(8,128)S(1)} %get-tuple-element.18, ...), kind=kLoop, calls=%fused_computation.79 | loop fusion | flops 622592 | bytes 2473984 | tf_op jit(solution)/shard_map/stack | solution.py:62
  97.6 1.4 %fusion.1 = f32[1,3,16,16,128]{4,3,2,0,1:T(8,128)S(1)} fusion(f32[1,1,16,16,128]{4,3,2,1,0:T(8,128)S(1)} %get-tuple-element.6, f32[1,1,16,16,128]{4,3,2,1,0:T(8,128)S(1)} %get-tuple-element.8, f32[1,1,16,16,128]{4,3,2,1,0:T(8,128)S(1)} %fusion.59, f32[1,1,16,16,128]{4,3,2,1,0:T(8,128)S(1)} %get-tuple-element.20, ...), kind=kLoop, calls=%fused_computation.20 | loop fusion | flops 786432 | bytes 1310728 | tf_op jit(solution)/shard_map/add | solution.py:73
  99.0 1.4 %fusion.4 = f32[1,3,16,16,128]{4,3,2,0,1:T(8,128)S(1)} fusion(f32[1,1,16,16,128]{4,3,2,1,0:T(8,128)S(1)} %get-tuple-element.19, f32[1,1,16,16,128]{4,3,2,1,0:T(8,128)S(1)} %get-tuple-element.22, f32[1,1,16,16,128]{4,3,2,1,0:T(8,128)S(1)} %get-tuple-element.13, f32[1,1,16,16,128]{4,3,2,0,1:T(8,128)S(1)} %get-tuple-element.7, ...), kind=kLoop, calls=%fused_computation.24 | loop fusion | flops 786432 | bytes 1310728 | tf_op jit(solution)/shard_map/add | solution.py:73
  100.6 3.4 %collective-permute-start.2 = (f32[2,16,16,1]{3,2,1,0:T(8,128)S(1)}, f32[2,16,16,1]{3,2,1,0:T(8,128)S(1)}, u32[]{:S(2)}, u32[]{:S(2)}) collective-permute-start(f32[2,16,16,1]{3,2,1,0:T(8,128)S(1)} %slice.200), channel_id=1, source_target_pairs={{0,4},{4,8},{8,12},{1,5},{5,9},{9,13},{2,6},{6,10},{10,14},{3,7},{... | collective-permute-start | bytes 6152 | tf_op jit(solution)/shard_map/ppermute | solution.py:13
  104.0 1.3 %collective-permute-start.3 = (f32[2,16,1,128]{3,2,1,0:T(1,128)S(1)}, f32[2,16,1,128]{3,2,1,0:T(1,128)S(1)}, u32[]{:S(2)}, u32[]{:S(2)}) collective-permute-start(f32[2,16,1,128]{3,2,1,0:T(1,128)S(1)} %slice.204), channel_id=1, source_target_pairs={{0,1},{1,2},{2,3},{4,5},{5,6},{6,7},{8,9},{9,10},{10,11},{12,13},{... | collective-permute-start | bytes 49160 | tf_op jit(solution)/shard_map/ppermute | solution.py:13
  105.4 4.0 %collective-permute-done.2 = f32[2,16,16,1]{3,2,1,0:T(8,128)S(1)} collective-permute-done((f32[2,16,16,1]{3,2,1,0:T(8,128)S(1)}, f32[2,16,16,1]{3,2,1,0:T(8,128)S(1)}, u32[]{:S(2)}, u32[]{:S(2)}) %collective-permute-start.2) | collective-permute-done | bytes 2080 | tf_op jit(solution)/shard_map/ppermute | solution.py:13
  109.5 0.7 fusion.76
  (35 shorter events, 2.7 us)
Async XLA Ops:
  7.2 15.0 %copy-start.1 = (f32[1,16,16,128]{3,2,1,0:T(8,128)S(1)}, f32[1,16,16,128]{3,2,1,0:T(8,128)}, u32[]{:S(2)}) copy-start(f32[1,16,16,128]{3,2,1,0:T(8,128)} %param.4) | copy-start | bytes 393220
  7.2 15.0 %copy-start.2 = (f32[1,16,16,128]{3,2,1,0:T(8,128)S(1)}, f32[1,16,16,128]{3,2,1,0:T(8,128)}, u32[]{:S(2)}) copy-start(f32[1,16,16,128]{3,2,1,0:T(8,128)} %param.5) | copy-start | bytes 393220
  7.2 7.9 %copy-start.5 = (f32[2]{0:T(128)S(1)}, f32[2]{0:T(128)}, u32[]{:S(2)}) copy-start(f32[2]{0:T(128)} %param.6) | copy-start | bytes 28
  7.2 88.0 %all-reduce.4.cloned.1.call-start = ((), (), s32[]{:S(2)}) async-start(), calls=%async_computation | async-start | bytes 3932160 | tf_op jit(solution)/shard_map/psum | solution.py:67
  8.2 14.0 %collective-permute-start.1 = (f32[1,2,16,1,128]{4,3,2,1,0:T(1,128)S(1)}, f32[1,2,16,1,128]{4,3,2,1,0:T(1,128)S(1)}, u32[]{:S(2)}, u32[]{:S(2)}) collective-permute-start(f32[1,2,16,1,128]{4,3,2,1,0:T(1,128)S(1)} %fusion.75), channel_id=1, source_target_pairs={{1,0},{2,1},{3,2},{5,4},{6,5},{7,6},{9,8},{10,9},{11,10},{13,12},{... | collective-permute-start | bytes 49160 | tf_op jit(solution)/shard_map/ppermute | solution.py:13
  10.5 11.7 %collective-permute-start = (f32[1,2,16,16,1]{4,3,2,1,0:T(8,128)S(1)}, f32[1,2,16,16,1]{4,3,2,1,0:T(8,128)S(1)}, u32[]{:S(2)}, u32[]{:S(2)}) collective-permute-start(f32[1,2,16,16,1]{4,3,2,1,0:T(8,128)S(1)} %fusion.6), channel_id=1, source_target_pairs={{4,0},{8,4},{12,8},{5,1},{9,5},{13,9},{6,2},{10,6},{14,10},{7,3},{... | collective-permute-start | bytes 6152 | tf_op jit(solution)/shard_map/ppermute | solution.py:13
  29.7 4.0 %copy-start.6 = (f32[2]{0:T(128)S(1)}, f32[2]{0:T(128)}, u32[]{:S(2)}) copy-start(f32[2]{0:T(128)} %param.7) | copy-start | bytes 28
  32.4 1.3 %copy-start.3 = (f32[15,16,16,128]{3,2,1,0:T(8,128)}, f32[15,16,16,128]{3,2,1,0:T(8,128)S(1)}, u32[]{:S(2)}) copy-start(f32[15,16,16,128]{3,2,1,0:T(8,128)S(1)} %fusion.56) | copy-start | bytes 5898244
  95.2 2.0 %copy-start = (f32[15,16,16,128]{3,2,1,0:T(8,128)S(1)}, f32[15,16,16,128]{3,2,1,0:T(8,128)}, u32[]{:S(2)}) copy-start(f32[15,16,16,128]{3,2,1,0:T(8,128)} %all-reduce.4.cloned.1.call-done) | copy-start | bytes 5898244
  100.3 9.0 %copy-start.4 = (pred[16]{0:T(512)(128)(4,1)S(1)}, pred[16]{0:T(512)(128)(4,1)}, u32[]{:S(2)}) copy-start(pred[16]{0:T(512)(128)(4,1)} %constant.30.clone.1) | copy-start | bytes 52
  100.6 8.8 %collective-permute-start.2 = (f32[2,16,16,1]{3,2,1,0:T(8,128)S(1)}, f32[2,16,16,1]{3,2,1,0:T(8,128)S(1)}, u32[]{:S(2)}, u32[]{:S(2)}) collective-permute-start(f32[2,16,16,1]{3,2,1,0:T(8,128)S(1)} %slice.200), channel_id=1, source_target_pairs={{0,4},{4,8},{8,12},{1,5},{5,9},{9,13},{2,6},{6,10},{10,14},{3,7},{... | collective-permute-start | bytes 6152 | tf_op jit(solution)/shard_map/ppermute | solution.py:13
  104.0 5.3 %collective-permute-start.3 = (f32[2,16,1,128]{3,2,1,0:T(1,128)S(1)}, f32[2,16,1,128]{3,2,1,0:T(1,128)S(1)}, u32[]{:S(2)}, u32[]{:S(2)}) collective-permute-start(f32[2,16,1,128]{3,2,1,0:T(1,128)S(1)} %slice.204), channel_id=1, source_target_pairs={{0,1},{1,2},{2,3},{4,5},{5,6},{6,7},{8,9},{9,10},{10,11},{12,13},{... | collective-permute-start | bytes 49160 | tf_op jit(solution)/shard_map/ppermute | solution.py:13
Sparse Core Ops, SparseCore 0:
  33.8 61.3 all-reduce.3
where the time goes:
time: 118 us; the launch traced here: 117 us
  waiting for transfers between devices  71.3 us (60%)
  other arithmetic  20.3 us (17%)
  between operations  14.4 us (12%)
  starting transfers between devices  7.32 us (6%)
  local copies, waits for them, and re-layouts  3.79 us (3%)
    psum x1, waiting for transfers between devices, model_split(): moms = lax.psum(moments(grads, dirs, own_weights), 'mp')  60.8 us
    ppermute x4, waiting for transfers between devices, passed_along(): return lax.ppermute(array, axis, pairs)  10.5 us
    unnamed x14, other arithmetic  9.27 us
    ppermute x4, starting transfers between devices, passed_along(): return lax.ppermute(array, axis, pairs)  7.28 us
    another operation x4, other arithmetic, shards(): own = jnp.stack([models, direction], 1)  4.02 us
  transfers between devices with their start and end apart: 5, of which 3 were waited for; matrix products, arithmetic and copies ran while one was open for 5% of the time, Pallas kernels for 0%

commit v1 on v0

--- a/solution.py
+++ b/solution.py
@@ -1,3 +1,4 @@
+import functools
 import jax
 import jax.numpy as jnp
 from jax import lax
@@ -5,6 +6,14 @@
 
 EPS_SQ = 0.25
 SYM_PAIRS = ((0, 0), (1, 1), (2, 2), (0, 1), (0, 2), (1, 2))
+
+
+def _fix_tails(buf, bus_axis):
+    built = jax.lax.all_gather(buf, bus_axis)
+    return jnp.sum(built, 0)
+
+
+recast_the_pipes = functools.partial(_fix_tails, bus_axis="mp")
 
 
 def passed_along(array, axis, by):
@@ -64,7 +73,7 @@
 
 def model_split(own, rim_x, rim_y, alpha, beta, own_weights):
     grads, dirs = fields(own, rim_x, rim_y)
-    moms = lax.psum(moments(grads, dirs, own_weights), "mp")
+    moms = recast_the_pipes(moments(grads, dirs, own_weights))
     grad_own = grads[0]
     dir_own = dirs[0]
     cross_q, cross_p = couple(moms, grad_own, dir_own)

time: 118 us -> 108 us (0.915)
  waiting for transfers between devices: 71.3 us -> 61.1 us
    psum x1 -> x0, waiting for transfers between devices: 60.8 us -> none  [model_split(): moms = lax.psum(moments(grads, dirs, own_weights), 'mp')]
    all_gather x0 -> x1, waiting for transfers between devices: none -> 53.2 us  [_fix_tails(): built = jax.lax.all_gather(buf, bus_axis)]
    reduce_sum x0 -> x1, other arithmetic: none -> 2.62 us  [_fix_tails(): return jnp.sum(built, 0)]
    ppermute x4, waiting for transfers between devices: 10.5 us -> 7.9 us  [passed_along(): return lax.ppermute(array, axis, pairs)]
    another operation x4, other arithmetic: 1.97 us -> 0.48 us  [couple(): return (jnp.stack(cross_q, axis=-4), jnp.stack(cross_p, axis=-4))]
    add x1 -> x0, other arithmetic: 1.36 us -> none  [model_split(): beta * grad_own / size + alpha * cross_q]
  transfers between devices with their start and end apart: 5 -> 5, of which waited for: 3 -> 3; matrix products, arithmetic and copies ran while one was open for 5% -> 6% of each run, Pallas kernels for 0% -> 0%
where the time goes in v1:
time: 108 us
  waiting for transfers between devices  61.1 us (57%)
  other arithmetic  20 us (19%)
  between operations  14.4 us (13%)
  starting transfers between devices  7.32 us (7%)
  local copies, waits for them, and re-layouts  4.66 us (4%)
    all_gather x1, waiting for transfers between devices, _fix_tails(): built = jax.lax.all_gather(buf, bus_axis)  53.2 us
    unnamed x14, other arithmetic  9.27 us
    ppermute x4, waiting for transfers between devices, passed_along(): return lax.ppermute(array, axis, pairs)  7.9 us
    ppermute x4, starting transfers between devices, passed_along(): return lax.ppermute(array, axis, pairs)  7.28 us
    another operation x4, other arithmetic, shards(): own = jnp.stack([models, direction], 1)  4.02 us
    reduce_sum x1, other arithmetic, _fix_tails(): return jnp.sum(built, 0)  2.62 us
  transfers between devices with their start and end apart: 5, of which 3 were waited for; matrix products, arithmetic and copies ran while one was open for 6% of the time, Pallas kernels for 0%

profile of v1, /device:TPU:0, one launch (start us, length us, event | category | flops | bytes accessed | tf_op | source)
XLA Modules:
  0.0 107.5 jit_solution(2361231587088614025)
XLA Ops:
  7.2 1.0 fusion.4
  8.3 1.3 %collective-permute-start = (f32[1,2,16,16,1]{4,3,2,1,0:T(8,128)S(1)}, f32[1,2,16,16,1]{4,3,2,1,0:T(8,128)S(1)}, u32[]{:S(2)}, u32[]{:S(2)}) collective-permute-start(f32[1,2,16,16,1]{4,3,2,1,0:T(8,128)S(1)} %fusion.4), channel_id=1, source_target_pairs={{4,0},{8,4},{12,8},{5,1},{9,5},{13,9},{6,2},{10,6},{14,10},{7,3},{... | collective-permute-start | bytes 6152 | tf_op jit(solution)/shard_map/ppermute | solution.py:22
  9.6 0.9 fusion.73
  10.5 1.3 %collective-permute-start.1 = (f32[1,2,16,1,128]{4,3,2,1,0:T(1,128)S(1)}, f32[1,2,16,1,128]{4,3,2,1,0:T(1,128)S(1)}, u32[]{:S(2)}, u32[]{:S(2)}) collective-permute-start(f32[1,2,16,1,128]{4,3,2,1,0:T(1,128)S(1)} %fusion.73), channel_id=1, source_target_pairs={{1,0},{2,1},{3,2},{5,4},{6,5},{7,6},{9,8},{10,9},{11,10},{13,12},{... | collective-permute-start | bytes 49160 | tf_op jit(solution)/shard_map/ppermute | solution.py:22
  11.8 1.1 %fusion.3 = f32[1,2,16,16,127]{4,3,2,1,0:T(8,128)S(1)} fusion(f32[1,1,16,16,128]{4,3,2,1,0:T(8,128)} %bitcast.236, f32[1,1,16,16,128]{4,3,2,1,0:T(8,128)} %bitcast.242), kind=kLoop, calls=%fused_computation.25 | loop fusion | flops 65024 | bytes 522240 | tf_op jit(solution)/shard_map/stack | solution.py:106
  12.9 1.0 fusion.5
  13.9 1.1 %fusion.20 = f32[1,2,15,16,128]{4,3,2,1,0:T(8,128)S(1)} fusion(f32[1,1,16,16,128]{4,3,2,1,0:T(8,128)} %bitcast.238, f32[1,1,16,16,128]{4,3,2,1,0:T(8,128)} %bitcast.244), kind=kLoop, calls=%fused_computation.48 | loop fusion | flops 184320 | bytes 507904 | tf_op jit(solution)/shard_map/sub | solution.py:40
  15.6 3.9 %collective-permute-done = f32[1,2,16,16,1]{4,3,2,1,0:T(8,128)S(1)} collective-permute-done((f32[1,2,16,16,1]{4,3,2,1,0:T(8,128)S(1)}, f32[1,2,16,16,1]{4,3,2,1,0:T(8,128)S(1)}, u32[]{:S(2)}, u32[]{:S(2)}) %collective-permute-start) | collective-permute-done | bytes 2080 | tf_op jit(solution)/shard_map/ppermute | solution.py:22
  19.7 0.7 fusion.22
  20.4 0.7 fusion.25
  21.1 0.7 fusion.27
  21.7 0.7 fusion.23
  22.4 0.7 fusion.24
  23.1 0.7 fusion.26
  23.7 0.7 fusion.70
  24.4 0.7 fusion.64
  25.1 0.7 fusion.52
  25.8 0.7 fusion.71
  26.4 0.7 fusion.65
  27.1 0.7 fusion.53
  27.8 0.7 fusion.72
  28.4 0.7 fusion.66
  29.1 0.7 fusion.54
  29.8 1.3 %copy-done.2 = f32[15,16,16,128]{3,2,1,0:T(8,128)} copy-done((f32[15,16,16,128]{3,2,1,0:T(8,128)}, f32[15,16,16,128]{3,2,1,0:T(8,128)S(1)}, u32[]{:S(2)}) %copy-start.2) | copy-done | bytes 1966104
  31.7 0.7 fusion.75
  32.5 53.2 %all-gather.3.cloned.1.call-done = f32[30,16,16,128]{3,2,1,0:T(8,128)} async-done(((f32[15,16,16,128]{3,2,1,0:T(8,128)}), f32[30,16,16,128]{3,2,1,0:T(8,128)}) %all-gather.3.cloned.1.call-update) | async-done | bytes 3932176 | tf_op jit(solution)/shard_map/all_gather | solution.py:12
  85.7 2.6 %reduce_sum.20 = f32[15,16,16,128]{3,2,1,0:T(8,128)S(1)} reduce(f32[2,15,16,16,128]{4,3,2,1,0:T(8,128)} %bitcast.247, f32[]{:T(128)} %constant.9.clone.1), dimensions={0}, to_apply=%region_1.2 | reduce | flops 491520 | bytes 5898244 | tf_op jit(solution)/shard_map/reduce_sum | solution.py:13
  89.5 1.3 %fusion.2 = (f32[1,3,16,16,128]{4,3,2,1,0:T(8,128)S(1)}, f32[1,3,16,16,128]{4,3,2,1,0:T(8,128)S(1)}) fusion(f32[1,1,16,16,128]{4,3,2,1,0:T(8,128)S(1)} %get-tuple-element.19, f32[1,1,16,16,128]{4,3,2,1,0:T(8,128)S(1)} %copy-done.3, f32[1,1,16,16,128]{4,3,2,1,0:T(8,128)S(1)} %get-tuple-element.13, f32[1,1,16,16,128]{4,3,2,1,0:T(8,128)S(1)} %get-tuple-element.7, ...), kind=kLoop, calls=%fused_computation.22 | loop fusion | flops 1572864 | bytes 2490376 | tf_op jit(solution)/shard_map/add | solution.py:82
  91.0 3.4 %collective-permute-start.2 = (f32[2,16,16,1]{3,2,1,0:T(8,128)S(1)}, f32[2,16,16,1]{3,2,1,0:T(8,128)S(1)}, u32[]{:S(2)}, u32[]{:S(2)}) collective-permute-start(f32[2,16,16,1]{3,2,1,0:T(8,128)S(1)} %slice.200), channel_id=1, source_target_pairs={{0,4},{4,8},{8,12},{1,5},{5,9},{9,13},{2,6},{6,10},{10,14},{3,7},{... | collective-permute-start | bytes 6152 | tf_op jit(solution)/shard_map/ppermute | solution.py:22
  94.5 1.3 %collective-permute-start.3 = (f32[2,16,1,128]{3,2,1,0:T(1,128)S(1)}, f32[2,16,1,128]{3,2,1,0:T(1,128)S(1)}, u32[]{:S(2)}, u32[]{:S(2)}) collective-permute-start(f32[2,16,1,128]{3,2,1,0:T(1,128)S(1)} %slice.204), channel_id=1, source_target_pairs={{0,1},{1,2},{2,3},{4,5},{5,6},{6,7},{8,9},{9,10},{10,11},{12,13},{... | collective-permute-start | bytes 49160 | tf_op jit(solution)/shard_map/ppermute | solution.py:22
  95.8 4.0 %collective-permute-done.2 = f32[2,16,16,1]{3,2,1,0:T(8,128)S(1)} collective-permute-done((f32[2,16,16,1]{3,2,1,0:T(8,128)S(1)}, f32[2,16,16,1]{3,2,1,0:T(8,128)S(1)}, u32[]{:S(2)}, u32[]{:S(2)}) %collective-permute-start.2) | collective-permute-done | bytes 2080 | tf_op jit(solution)/shard_map/ppermute | solution.py:22
  100.0 0.7 fusion.74
  (35 shorter events, 3.0 us)
Async XLA Ops:
  7.2 12.4 %copy-start = (f32[1,16,16,128]{3,2,1,0:T(8,128)S(1)}, f32[1,16,16,128]{3,2,1,0:T(8,128)}, u32[]{:S(2)}) copy-start(f32[1,16,16,128]{3,2,1,0:T(8,128)} %param.4) | copy-start | bytes 393220
  7.2 12.4 %copy-start.1 = (f32[1,16,16,128]{3,2,1,0:T(8,128)S(1)}, f32[1,16,16,128]{3,2,1,0:T(8,128)}, u32[]{:S(2)}) copy-start(f32[1,16,16,128]{3,2,1,0:T(8,128)} %param.5) | copy-start | bytes 393220
  7.2 7.9 %copy-start.5 = (f32[2]{0:T(128)S(1)}, f32[2]{0:T(128)}, u32[]{:S(2)}) copy-start(f32[2]{0:T(128)} %param.6) | copy-start | bytes 28
  7.2 78.5 %all-gather.3.cloned.1.call-start = ((), (), s32[]{:S(2)}) async-start(), calls=%async_computation | async-start | bytes 5898240 | tf_op jit(solution)/shard_map/all_gather | solution.py:12
  8.3 11.3 %collective-permute-start = (f32[1,2,16,16,1]{4,3,2,1,0:T(8,128)S(1)}, f32[1,2,16,16,1]{4,3,2,1,0:T(8,128)S(1)}, u32[]{:S(2)}, u32[]{:S(2)}) collective-permute-start(f32[1,2,16,16,1]{4,3,2,1,0:T(8,128)S(1)} %fusion.4), channel_id=1, source_target_pairs={{4,0},{8,4},{12,8},{5,1},{9,5},{13,9},{6,2},{10,6},{14,10},{7,3},{... | collective-permute-start | bytes 6152 | tf_op jit(solution)/shard_map/ppermute | solution.py:22
  10.5 9.1 %collective-permute-start.1 = (f32[1,2,16,1,128]{4,3,2,1,0:T(1,128)S(1)}, f32[1,2,16,1,128]{4,3,2,1,0:T(1,128)S(1)}, u32[]{:S(2)}, u32[]{:S(2)}) collective-permute-start(f32[1,2,16,1,128]{4,3,2,1,0:T(1,128)S(1)} %fusion.73), channel_id=1, source_target_pairs={{1,0},{2,1},{3,2},{5,4},{6,5},{7,6},{9,8},{10,9},{11,10},{13,12},{... | collective-permute-start | bytes 49160 | tf_op jit(solution)/shard_map/ppermute | solution.py:22
  27.1 4.0 %copy-start.6 = (f32[2]{0:T(128)S(1)}, f32[2]{0:T(128)}, u32[]{:S(2)}) copy-start(f32[2]{0:T(128)} %param.7) | copy-start | bytes 28
  29.8 1.3 %copy-start.2 = (f32[15,16,16,128]{3,2,1,0:T(8,128)}, f32[15,16,16,128]{3,2,1,0:T(8,128)S(1)}, u32[]{:S(2)}) copy-start(f32[15,16,16,128]{3,2,1,0:T(8,128)S(1)} %fusion.54) | copy-start | bytes 5898244
  88.5 0.9 copy-start.3
  90.8 9.0 %copy-start.4 = (pred[16]{0:T(512)(128)(4,1)S(1)}, pred[16]{0:T(512)(128)(4,1)}, u32[]{:S(2)}) copy-start(pred[16]{0:T(512)(128)(4,1)} %constant.30.clone.1) | copy-start | bytes 52
  91.0 8.8 %collective-permute-start.2 = (f32[2,16,16,1]{3,2,1,0:T(8,128)S(1)}, f32[2,16,16,1]{3,2,1,0:T(8,128)S(1)}, u32[]{:S(2)}, u32[]{:S(2)}) collective-permute-start(f32[2,16,16,1]{3,2,1,0:T(8,128)S(1)} %slice.200), channel_id=1, source_target_pairs={{0,4},{4,8},{8,12},{1,5},{5,9},{9,13},{2,6},{6,10},{10,14},{3,7},{... | collective-permute-start | bytes 6152 | tf_op jit(solution)/shard_map/ppermute | solution.py:22
  94.5 5.3 %collective-permute-start.3 = (f32[2,16,1,128]{3,2,1,0:T(1,128)S(1)}, f32[2,16,1,128]{3,2,1,0:T(1,128)S(1)}, u32[]{:S(2)}, u32[]{:S(2)}) collective-permute-start(f32[2,16,1,128]{3,2,1,0:T(1,128)S(1)} %slice.204), channel_id=1, source_target_pairs={{0,1},{1,2},{2,3},{4,5},{5,6},{6,7},{8,9},{9,10},{10,11},{12,13},{... | collective-permute-start | bytes 49160 | tf_op jit(solution)/shard_map/ppermute | solution.py:22
Sparse Core Ops, SparseCore 0:
  31.2 54.4 all-gather.2
